TPU v7x, 256 devices: a whole 4x4x8 slice. The times are simulated.
256 devices in a mesh: seq: 32 (over x, z), head: 8 (over y, core).
Axes of the slice: x: 4, y: 4, z: 8, core: 2. Of those that a mesh axis runs over, the one named last changes fastest.
Arguments:
- queries: bfloat16 [16384, 8192], P('seq', 'head'), may hold values from -48 to 48
- keys: bfloat16 [16384, 1024], P('seq', 'head'), may hold values from -48 to 48
- values: bfloat16 [16384, 1024], P('seq', 'head'), may hold values from -6 to 6
- offsets: int32 [64], P('seq'), may hold values from 0 to 24064, as said below
- query_map: bfloat16 [64, 128, 64], P('head'), may hold values from -0.5 to 0.5
- key_map: bfloat16 [64, 128, 64], P('head'), may hold values from -0.5 to 0.5
- window_logit: float32 [64], P('head'), may hold values from -2 to 6
Outputs:
- attn_rows: bfloat16 [16384, 8192], P(('seq', 'head'))
Inputs may be any that keep to these rules, and one draw needn't show every extreme that they name: offsets[0] = 0, and each span's offset exceeds the one before by 256 or 512.
All inputs are finite; a program needn't handle non-finite values.
Results may differ from a plain program's by a relative error of at most 0.004.
The roundings to bfloat16 on the way count: a program that leaves them out, or rounds other values in their place, can miss the bound.
Values may be sent and summed in bfloat16 or wider, within the bound.
No kernel may reach another device: no remote copies, remote signals or barrier semaphores. Data moves between devices by JAX's collectives and lax.ppermute only.
A program may use at most 128 MiB of HBM per device.

v0:
```python
import math
import jax
import jax.numpy as jnp
from jax import lax
from jax.sharding import PartitionSpec as P

WINDOW = 64
BLOCK = 512
SPAN = 256


def passed_along(value, axis, steps):
    names = axis if isinstance(axis, tuple) else (axis,)
    count = math.prod((lax.axis_size(name) for name in names))
    first, last = (max(0, -steps), min(count, count - steps))
    return lax.ppermute(value, axis, [(source, source + steps) for source in range(first, last)])


def angle_tables(positions, half):
    frequency = [500000.0 ** (-float(order) / half) for order in range(half)]
    coarse = jnp.asarray([4096.0 * value % (2.0 * math.pi) for value in frequency], jnp.float32)
    medium = jnp.asarray([64.0 * value % (2.0 * math.pi) for value in frequency], jnp.float32)
    finest = jnp.asarray(frequency, jnp.float32)
    upper = (positions // 4096).astype(jnp.float32)[:, None] * coarse[None, :]
    middle = (positions // 64 % 64).astype(jnp.float32)[:, None] * medium[None, :]
    lower = (positions % 64).astype(jnp.float32)[:, None] * finest[None, :]
    cos_high = jnp.cos(upper) * jnp.cos(middle) - jnp.sin(upper) * jnp.sin(middle)
    sin_high = jnp.sin(upper) * jnp.cos(middle) + jnp.cos(upper) * jnp.sin(middle)
    cosine = cos_high * jnp.cos(lower) - sin_high * jnp.sin(lower)
    sine = sin_high * jnp.cos(lower) + cos_high * jnp.sin(lower)
    return (cosine, sine)


def rotate(rows, cosine, sine):
    half = rows.shape[-1] // 2
    first = rows[..., :half]
    second = rows[..., half:]
    cos_rows = cosine[:, None, :]
    sin_rows = sine[:, None, :]
    return jnp.concatenate(
        [first * cos_rows - second * sin_rows, second * cos_rows + first * sin_rows], axis=-1
    )


def two_softmax(logits):
    return jnp.concatenate(
        [jax.nn.softmax(logits, axis=-1), jax.nn.softmax(-logits, axis=-1)], axis=-1
    )


def split_parts(full_value):
    high_part = full_value.astype(jnp.bfloat16)
    rest_part = (full_value - high_part.astype(jnp.float32)).astype(jnp.bfloat16)
    return (high_part, rest_part)


def body(queries, keys, values, offsets, query_map, key_map, window_logit):
    tokens = queries.shape[0]
    heads = query_map.shape[0]
    head_dim = query_map.shape[1]
    feat = query_map.shape[2]
    kv_local = keys.shape[1] // head_dim
    group = heads // kv_local
    blocks = tokens // BLOCK
    extent = BLOCK + WINDOW
    positions = (offsets[:, None] + jnp.arange(SPAN, dtype=jnp.int32)[None, :]).reshape(tokens)
    cosine, sine = angle_tables(positions, head_dim // 2)
    rot_k = rotate(
        keys.reshape(tokens, kv_local, head_dim).astype(jnp.float32), cosine, sine
    ).astype(jnp.bfloat16)
    value_rows = values.reshape(tokens, kv_local, head_dim)
    tail_keys, tail_values = passed_along(
        (rot_k[tokens - WINDOW :], value_rows[tokens - WINDOW :]), ("sx", "sz"), 1
    )
    ext_keys = jnp.concatenate([tail_keys, rot_k], axis=0)
    ext_values = jnp.concatenate([tail_values, value_rows], axis=0)
    valid = (
        (jnp.arange(tokens + WINDOW) >= WINDOW)
        | (lax.axis_index("sx") > 0)
        | (lax.axis_index("sz") > 0)
    )
    grouped_map = key_map.reshape(kv_local, group, head_dim, feat)
    key_logits = jnp.einsum(
        "ngd,gkdf->ngkf", ext_keys, grouped_map, preferred_element_type=jnp.float32
    )
    phi_key = jnp.where(valid[:, None, None, None], two_softmax(key_logits), 0.0).astype(
        jnp.bfloat16
    )
    lag_phi = phi_key[:tokens].reshape(blocks, BLOCK, kv_local, group, 2 * feat)
    lag_values = ext_values[:tokens].reshape(blocks, BLOCK, kv_local, head_dim)
    block_states = jnp.einsum(
        "bjgkf,bjgd->bgkfd", lag_phi, lag_values, preferred_element_type=jnp.float32
    )
    block_norms = jnp.sum(lag_phi, axis=1, dtype=jnp.float32)
    total_state = jnp.sum(block_states, axis=0)
    total_norm = jnp.sum(block_norms, axis=0)
    before_state = jnp.concatenate(
        [jnp.zeros_like(block_states), jnp.cumsum(block_states, axis=0)[:-1]], axis=0
    )
    before_norm = jnp.concatenate(
        [jnp.zeros_like(block_norms), jnp.cumsum(block_norms, axis=0)[:-1]], axis=0
    )
    state_shape = total_state.shape
    state_size = total_state.size
    packed = jnp.concatenate([total_state.reshape(-1), total_norm.reshape(-1)])

    def exclusive_scan(value, axis):
        count = lax.axis_size(axis)
        inclusive = value
        exclusive = jnp.zeros_like(value)
        first = None
        steps = 1
        while steps < count:
            received = passed_along(inclusive, axis, steps)
            first = received if first is None else first
            exclusive = exclusive + received
            if 2 * steps < count:
                inclusive = inclusive + received
            steps *= 2
        return (exclusive, first)

    row_total = lax.psum(packed, "sz")
    inner, first_received = exclusive_scan(packed, "sz")
    outer, _ = exclusive_scan(row_total, "sx")
    exclusive = inner + outer
    queries, first_received = lax.optimization_barrier((queries, first_received))
    rot_q = rotate(
        queries.reshape(tokens, heads, head_dim).astype(jnp.float32), cosine, sine
    ).astype(jnp.bfloat16)
    query_logits = jnp.einsum("nhd,hdf->nhf", rot_q, query_map, preferred_element_type=jnp.float32)
    phi_query = (
        two_softmax(query_logits).astype(jnp.bfloat16).reshape(tokens, kv_local, group, 2 * feat)
    )
    prior_state = exclusive[:state_size].reshape(state_shape)
    prior_norm = exclusive[state_size:].reshape(total_norm.shape)
    factor = jax.nn.sigmoid(window_logit).reshape(kv_local, group)
    rot_grouped = rot_q.reshape(tokens, kv_local, group, head_dim)
    row_index = jnp.arange(BLOCK)[:, None]
    col_index = jnp.arange(extent)[None, :]
    window_mask = (col_index > row_index) & (col_index <= row_index + WINDOW)
    linear_mask = col_index <= row_index
    live = valid[None, :]
    scores = jnp.einsum(
        "igkd,jgd->gkij", rot_grouped, ext_keys, preferred_element_type=jnp.float32
    ) / math.sqrt(head_dim)
    near_window = window_mask & live
    peak = jnp.max(jnp.where(near_window, scores, -jnp.inf), axis=-1, keepdims=True)
    weights = jnp.where(near_window, jnp.exp(scores - peak), 0.0)
    window_sum = jnp.sum(weights, axis=-1)
    affinity = jnp.einsum("igkf,jgkf->gkij", phi_query, phi_key, preferred_element_type=jnp.float32)
    affinity = jnp.where(linear_mask & live, affinity, 0.0)
    near_sum = jnp.sum(affinity, axis=-1)
    window_num = jnp.einsum(
        "gkij,jgd->igkd",
        weights.astype(jnp.bfloat16),
        ext_values,
        preferred_element_type=jnp.float32,
    )
    near_num = jnp.einsum(
        "gkij,jgd->igkd",
        affinity.astype(jnp.bfloat16),
        ext_values,
        preferred_element_type=jnp.float32,
    )
    state_now = prior_state + before_state[0]
    norm_now = prior_norm + before_norm[0]
    state_high, state_rest = split_parts(state_now)
    norm_high, norm_rest = split_parts(norm_now)
    far_num = jnp.einsum(
        "igkf,gkfd->igkd", phi_query, state_high, preferred_element_type=jnp.float32
    )
    far_num = far_num + jnp.einsum(
        "igkf,gkfd->igkd", phi_query, state_rest, preferred_element_type=jnp.float32
    )
    far_sum = jnp.einsum("igkf,gkf->igk", phi_query, norm_high, preferred_element_type=jnp.float32)
    far_sum = far_sum + jnp.einsum(
        "igkf,gkf->igk", phi_query, norm_rest, preferred_element_type=jnp.float32
    )
    head_factor = factor[None, :, :, None]
    numerator = head_factor * window_num + (1.0 - head_factor) * (near_num + far_num)
    denominator = factor[None] * jnp.transpose(window_sum, (2, 0, 1)) + (1.0 - factor[None]) * (
        jnp.transpose(near_sum, (2, 0, 1)) + far_sum
    )
    outputs = (numerator / denominator[..., None]).astype(jnp.bfloat16)
    result = outputs.reshape(tokens, heads * head_dim)
    return lax.all_to_all(result, "head", split_axis=0, concat_axis=1, tiled=True)


def solution(mesh):
    seq_count = mesh.shape["seq"]
    inner = math.gcd(seq_count, 8)
    split_mesh = jax.sharding.Mesh(
        mesh.devices.reshape(seq_count // inner, inner, mesh.shape["head"]), ("sx", "sz", "head")
    )
    rows = ("sx", "sz")
    in_specs = (
        P(rows, "head"),
        P(rows, "head"),
        P(rows, "head"),
        P(rows),
        P("head", None, None),
        P("head", None, None),
        P("head"),
    )
    out_specs = P(("sx", "sz", "head"), None)
    return jax.shard_map(
        body, mesh=split_mesh, in_specs=in_specs, out_specs=out_specs, check_vma=False
    )
```

profile of v0, /device:TPU:160, one launch (start us, length us, event | category | flops | bytes accessed | tf_op | source)
XLA Modules:
  0.0 221.4 jit_solution(13633600873984047340)
XLA Ops:
  6.5 0.8 add_bitcast_fusion
  7.3 1.0 copy.37
  8.4 2.4 %subtract_convert_fusion.3 = (bf16[512,1,64]{0,2,1:T(8,128)(2,1)S(1)}, bf16[512,1,64]{0,2,1:T(8,128)(2,1)S(1)}) fusion(f32[512,1,128]{0,2,1:T(8,128)S(1)} %bitcast_convert_fusion, f32[64]{0:T(128)} %constant.80.clone, f32[512]{0:T(512)S(1)} %get-tuple-element.27, f32[64]{0:T(128)} %constant.79.clone, f32[512]{0:T(512)S(1)} %get-tuple-element.26, ...), kind=kLoop, calls=%fused_computation.118 | loop fusion | flops 753664 | bytes 400128 | tf_op jit(solution)/shard_map/convert.6
  10.8 2.9 %collective-permute-start.1 = (bf16[64,1,128]{0,2,1:T(8,128)(2,1)S(1)}, bf16[64,1,128]{0,2,1:T(8,128)(2,1)S(1)}, u32[]{:S(2)}, u32[]{:S(2)}) collective-permute-start(bf16[64,1,128]{0,2,1:T(8,128)(2,1)S(1)} %pad_maximum_fusion.13), channel_id=1, source_target_pairs={{0,8},{8,16},{16,24},{24,32},{32,40},{40,48},{48,56},{56,64},{64,7... | collective-permute-start | bytes 49160 | tf_op jit(solution)/shard_map/ppermute | solution.py:16
  13.8 0.7 slice_bitcast_fusion
  14.5 2.9 %collective-permute-start = (bf16[64,1,128]{2,0,1:T(8,128)(2,1)S(1)}, bf16[64,1,128]{2,0,1:T(8,128)(2,1)S(1)}, u32[]{:S(2)}, u32[]{:S(2)}) collective-permute-start(bf16[64,1,128]{2,0,1:T(8,128)(2,1)S(1)} %slice_bitcast_fusion), channel_id=1, source_target_pairs={{0,8},{8,16},{16,24},{24,32},{32,40},{40,48},{48,56},{56,64},{64,7... | collective-permute-start | bytes 49160 | tf_op jit(solution)/shard_map/ppermute | solution.py:16
  17.4 2.9 %fusion.64 = (f32[512,64]{0,1:T(8,128)}, f32[512,64]{0,1:T(8,128)}) fusion(f32[64]{0:T(128)} %constant.80.clone, f32[512]{0:T(512)S(1)} %get-tuple-element.27, f32[64]{0:T(128)} %constant.79.clone, f32[512]{0:T(512)S(1)} %get-tuple-element.26, f32[64]{0:T(128)} %constant.78.clone, f32[512]{0:T(512)S(1)} %get-tuple-element.25), kind=kLoop, calls=%fused_computation.105 | loop fusion | flops 491520 | bytes 269056 | tf_op jit(solution)/shard_map/sub | solution.py:29
  20.3 1.2 broadcast_subtract_fusion
  21.6 2.4 %fusion.58 = f32[576,512]{0,1} fusion(bf16[128,512]{0,1:T(8,128)(2,1)} %bitcast.177, bf16[512,1,64]{0,2,1:T(8,128)(2,1)S(1)} %get-tuple-element.22, bf16[512,1,64]{0,2,1:T(8,128)(2,1)S(1)} %get-tuple-element.21, bf16[64,1,128]{0,2,1:T(8,128)(2,1)S(1)} %collective-permute-done.1), kind=kOutput, calls=%fused_computation.99 | convolution fusion | flops 75939840 | bytes 1458176
  24.0 2.3 %copy.39 = f32[576,8,64]{2,1,0:T(8,128)S(1)} copy(f32[576,8,64]{0,2,1:T(8,128)} %bitcast.171) | data formatting | bytes 2359296 | tf_op jit(solution)/shard_map/ngd,gkdf->ngkf/dot_general | solution.py:83
  26.3 1.3 bitcast_reduce_fusion
  27.6 3.6 %fusion.25 = (f32[576,8]{1,0:T(8,128)S(1)}, f32[576,8]{1,0:T(8,128)S(1)}) fusion(f32[576,8,64]{2,1,0:T(8,128)S(1)} %copy.39, f32[576,8]{1,0:T(8,128)S(1)} %get-tuple-element.9, f32[576,8]{1,0:T(8,128)S(1)} %get-tuple-element.10), kind=kLoop, calls=%fused_computation.39 | loop fusion | flops 1465344 | bytes 1253376 | tf_op jit(solution)/shard_map/reduce_sum | solution.py:47
  31.2 3.1 %fusion.24 = (bf16[576,1,8,64]{3,2,0,1:T(8,128)(2,1)S(1)}, bf16[576,1,8,64]{3,2,0,1:T(8,128)(2,1)S(1)}) fusion(f32[576,8,64]{2,1,0:T(8,128)S(1)} %copy.39, f32[576,8]{1,0:T(8,128)S(1)} %get-tuple-element.7, f32[576,8]{1,0:T(8,128)S(1)} %get-tuple-element.9, f32[576,8]{1,0:T(8,128)S(1)} %get-tuple-element.8, f32[576,8]{1,0:T(8,128)S(1)} %get-tuple-element.10), kind=kLoop, calls=%fused_computation.38 | loop fusion | flops 2064384 | bytes 2433024 | tf_op jit(solution)/shard_map/div | solution.py:47
  34.3 4.0 %convert_reduce_fusion = (f32[8,128]{1,0:T(8,128)S(1)}, bf16[512,1,8,128]{3,2,0,1:T(8,128)(2,1)S(1)}) fusion(bf16[576,1,8,64]{3,2,0,1:T(8,128)(2,1)S(1)} %get-tuple-element.18, bf16[576,1,8,64]{3,2,0,1:T(8,128)(2,1)S(1)} %get-tuple-element.17, pred[512]{0:T(512)(128)(4,1)S(1)} %slice-done), kind=kLoop, calls=%fused_computation.34 | loop fusion | flops 3668992 | bytes 2232832 | tf_op jit(solution)/shard_map/reduce_sum | solution.py:94
  39.0 0.7 copy-done.11
  39.7 2.1 collective-permute-start.2
  41.8 0.6 iota_add_fusion
  42.3 1.7 copy.43
  44.1 1.7 copy.45
  45.8 1.8 fusion.33
  47.6 2.9 %fusion.14 = bf16[576,8,128]{2,1,0:T(8,128)(2,1)} fusion(bf16[576,8,64]{2,1,0:T(8,128)(2,1)S(1)} %bitcast.169, bf16[576,8,64]{2,1,0:T(8,128)(2,1)S(1)} %bitcast.168, pred[576]{0:T(1024)(128)(4,1)S(1)} %copy-done.26), kind=kLoop, calls=%fused_computation.18 | loop fusion | flops 2949120 | bytes 2359872 | tf_op jit(solution)/shard_map/convert_element_type | solution.py:86
  50.5 4.4 %collective-permute-done.2 = f32[132096]{0:T(1024)S(1)} collective-permute-done((f32[132096]{0:T(1024)S(1)}, f32[132096]{0:T(1024)S(1)}, u32[]{:S(2)}, u32[]{:S(2)}) %collective-permute-start.2) | collective-permute-done | bytes 528416 | tf_op jit(solution)/shard_map/ppermute | solution.py:16
  54.9 1.7 copy.41
  56.9 1.9 copy.65
  58.8 1.9 copy.66
  60.8 2.8 %subtract_convert_fusion = (bf16[512,8,64]{2,0,1:T(8,128)(2,1)S(1)}, bf16[512,8,64]{2,0,1:T(8,128)(2,1)S(1)}) fusion(f32[512,8,64]{2,0,1:T(8,128)} %copy.66, f32[512,8,64]{2,0,1:T(8,128)} %copy.65, f32[512,64]{1,0:T(8,128)S(1)} %copy-done.19, f32[512,64]{1,0:T(8,128)S(1)} %copy-done.18), kind=kLoop, calls=%fused_computation.33 | loop fusion | flops 2097152 | bytes 3407872 | tf_op jit(solution)/shard_map/convert.4
  63.6 0.9 fusion.111
  64.5 1.9 fusion.110
  66.4 2.1 fusion.107
  68.4 1.9 collective-permute-start.3
  70.4 3.5 %fusion.2 = (f32[8,512]{1,0:T(8,128)S(1)}, f32[576,512,8]{1,0,2:T(8,128)S(1)}) fusion(pred[512,576]{0,1:T(8,128)(4,1)} %get-tuple-element.29, bf16[512,8,64]{2,0,1:T(8,128)(2,1)S(1)} %get-tuple-element.16, bf16[512,8,64]{2,0,1:T(8,128)(2,1)S(1)} %get-tuple-element.15, bf16[512,1,64]{0,2,1:T(8,128)(2,1)S(1)} %copy-done.16, ...), kind=kOutput, calls=%fused_computation.4 | convolution fusion | flops 613593088 | bytes 10944512 | tf_op jit(solution)/shard_map/igkd,jgd->gkij/dot_general | solution.py:143
  73.9 3.7 %copy-done.1 = f32[576,512,8]{1,0,2:T(8,128)} copy-done((f32[576,512,8]{1,0,2:T(8,128)}, f32[576,512,8]{1,0,2:T(8,128)S(1)}, u32[]{:S(2)}) %copy-start.1) | copy-done | bytes 9437208
  77.6 1.9 fusion.5
  79.5 68.3 %all-reduce.2.cloned.1.call-done = f32[132096]{0:T(1024)} async-done(((f32[132096]{0:T(1024)}), f32[132096]{0:T(1024)}) %all-reduce.2.cloned.1.call-update) | async-done | bytes 528400 | tf_op jit(solution)/shard_map/psum | solution.py:122
  147.9 3.5 %collective-permute-start.5 = (f32[132096]{0:T(1024)}, f32[132096]{0:T(1024)S(1)}, u32[]{:S(2)}, u32[]{:S(2)}) collective-permute-start(f32[132096]{0:T(1024)} %all-reduce.2.cloned.1.call-done), channel_id=1, source_target_pairs={{0,64},{64,128},{128,192},{1,65},{65,129},{129,193},{2,66},{66,130... | collective-permute-start | bytes 1585160 | tf_op jit(solution)/shard_map/ppermute | solution.py:16
  151.4 7.1 %fusion.10 = f32[128,8,512]{2,0,1:T(8,128)} fusion(f32[576,512,8]{1,0,2:T(8,128)} %copy-done.1, f32[8,512]{1,0:T(8,128)S(1)} %get-tuple-element.34, pred[512,576]{0,1:T(8,128)(4,1)S(1)} %copy-done.7, bf16[64,1,128]{2,0,1:T(8,128)(2,1)S(1)} %copy-done.32, bf16[512,1,128]{2,0,1:T(8,128)(2,1)S(1)} %bitcast.182), kind=kOutput, calls=%fused_computation.14 | convolution fusion | flops 613711872 | bytes 11993088 | tf_op jit(solution)/shard_map/gkij,jgd->igkd/dot_general | solution.py:153
  158.6 1.3 add.179
  159.9 1.4 collective-permute-start.4
  161.4 4.8 %collective-permute-start.6 = (f32[132096]{0:T(1024)S(1)}, f32[132096]{0:T(1024)S(1)}, u32[]{:S(2)}, u32[]{:S(2)}) collective-permute-start(f32[132096]{0:T(1024)S(1)} %add.181), channel_id=1, source_target_pairs={{0,128},{64,192},{1,129},{65,193},{2,130},{66,194},{3,131},{67,195... | collective-permute-start | bytes 1585160 | tf_op jit(solution)/shard_map/ppermute | solution.py:16
  166.6 3.6 %select_reduce_fusion = (f32[8,512]{1,0:T(8,128)S(1)}, bf16[8,512,576]{1,2,0:T(8,128)(2,1)}) fusion(pred[512,576]{0,1:T(8,128)(4,1)S(1)} %copy-done.21, bf16[512,8,64]{0,2,1:T(8,128)(2,1)S(1)} %get-tuple-element.38, bf16[512,8,64]{0,2,1:T(8,128)(2,1)S(1)} %get-tuple-element.39, bf16[576,8,128]{2,1,0:T(8,128)(2,1)S(1)} %copy-done.12), kind=kOutput, calls=%fused_computation.7 | convolution fusion | flops 613150720 | bytes 7258112 | tf_op jit(solution)/shard_map/igkf,jgkf->gkij/dot_general | solution.py:150
  170.3 15.6 %collective-permute-done.4 = f32[132096]{0:T(1024)S(1)} collective-permute-done((f32[132096]{0:T(1024)S(1)}, f32[132096]{0:T(1024)S(1)}, u32[]{:S(2)}, u32[]{:S(2)}) %collective-permute-start.4) | collective-permute-done | bytes 528416 | tf_op jit(solution)/shard_map/ppermute | solution.py:16
  185.9 1.2 add_add_fusion
  188.8 0.5 copy-done.29
  190.0 0.7 copy-done.33
  190.7 1.4 fusion.21
  192.2 0.8 copy.53
  193.4 20.1 %all_to_all.19 = bf16[8,64,1024]{2,1,0:T(8,128)(2,1)S(1)} all-to-all(bf16[8,64,1024]{2,1,0:T(8,128)(2,1)S(1)} %all_to_all.14), channel_id=1, replica_groups=mesh['sx'=4,'sz'=8,'head'=8] {'head'}, dimensions={0} | all-to-all | bytes 2097152 | tf_op jit(solution)/shard_map/all_to_all | solution.py:186
  213.5 1.1 copy.67
  (95 shorter events, 4.3 us)
Async XLA Ops:
  6.5 57.1 %copy-start = (bf16[8,128,64]{1,2,0:T(8,128)(2,1)S(1)}, bf16[8,128,64]{1,2,0:T(8,128)(2,1)}, u32[]{:S(2)}) copy-start(bf16[8,128,64]{1,2,0:T(8,128)(2,1)} %param.14) | copy-start | bytes 393220
  10.7 13.2 %copy-start.13 = (bf16[512,1,64]{0,2,1:T(8,128)(2,1)}, bf16[512,1,64]{0,2,1:T(8,128)(2,1)S(1)}, u32[]{:S(2)}) copy-start(bf16[512,1,64]{0,2,1:T(8,128)(2,1)S(1)} %get-tuple-element.21) | copy-start | bytes 196612
  10.7 13.2 %copy-start.15 = (bf16[512,1,64]{0,2,1:T(8,128)(2,1)}, bf16[512,1,64]{0,2,1:T(8,128)(2,1)S(1)}, u32[]{:S(2)}) copy-start(bf16[512,1,64]{0,2,1:T(8,128)(2,1)S(1)} %get-tuple-element.22) | copy-start | bytes 196612
  10.8 10.7 %collective-permute-start.1 = (bf16[64,1,128]{0,2,1:T(8,128)(2,1)S(1)}, bf16[64,1,128]{0,2,1:T(8,128)(2,1)S(1)}, u32[]{:S(2)}, u32[]{:S(2)}) collective-permute-start(bf16[64,1,128]{0,2,1:T(8,128)(2,1)S(1)} %pad_maximum_fusion.13), channel_id=1, source_target_pairs={{0,8},{8,16},{16,24},{24,32},{32,40},{40,48},{48,56},{56,64},{64,7... | collective-permute-start | bytes 49160 | tf_op jit(solution)/shard_map/ppermute | solution.py:16
  14.5 23.9 %collective-permute-start = (bf16[64,1,128]{2,0,1:T(8,128)(2,1)S(1)}, bf16[64,1,128]{2,0,1:T(8,128)(2,1)S(1)}, u32[]{:S(2)}, u32[]{:S(2)}) collective-permute-start(bf16[64,1,128]{2,0,1:T(8,128)(2,1)S(1)} %slice_bitcast_fusion), channel_id=1, source_target_pairs={{0,8},{8,16},{16,24},{24,32},{32,40},{40,48},{48,56},{56,64},{64,7... | collective-permute-start | bytes 49160 | tf_op jit(solution)/shard_map/ppermute | solution.py:16
  21.6 4.7 %copy-start.25 = (pred[576]{0:T(1024)(128)(4,1)}, pred[576]{0:T(1024)(128)(4,1)S(1)}, u32[]{:S(2)}) copy-start(pred[576]{0:T(1024)(128)(4,1)S(1)} %fusion.85) | copy-start | bytes 1732
  21.6 2.4 %copy-start.23 = (bf16[64,1,128]{0,2,1:T(8,128)(2,1)}, bf16[64,1,128]{0,2,1:T(8,128)(2,1)S(1)}, u32[]{:S(2)}) copy-start(bf16[64,1,128]{0,2,1:T(8,128)(2,1)S(1)} %collective-permute-done.1) | copy-start | bytes 49156
  31.2 3.2 %slice-start = ((pred[576]{0:T(1024)(128)(4,1)}), pred[512]{0:T(512)(128)(4,1)S(1)}, s32[]{:S(2)}) async-start(pred[576]{0:T(1024)(128)(4,1)} %copy-done.25), calls=%async_computation.2 | async-start | bytes 1024 | tf_op jit(solution)/shard_map/slice | solution.py:89
  34.3 4.5 %copy-start.2 = (bf16[576,1,8,64]{3,2,0,1:T(8,128)(2,1)}, bf16[576,1,8,64]{3,2,0,1:T(8,128)(2,1)S(1)}, u32[]{:S(2)}) copy-start(bf16[576,1,8,64]{3,2,0,1:T(8,128)(2,1)S(1)} %get-tuple-element.17) | copy-start | bytes 1769476
  34.3 4.5 %copy-start.4 = (bf16[576,1,8,64]{3,2,0,1:T(8,128)(2,1)}, bf16[576,1,8,64]{3,2,0,1:T(8,128)(2,1)S(1)}, u32[]{:S(2)}) copy-start(bf16[576,1,8,64]{3,2,0,1:T(8,128)(2,1)S(1)} %get-tuple-element.18) | copy-start | bytes 1769476
  34.3 4.0 %copy-start.27 = (bf16[512,128]{1,0:T(8,128)(2,1)S(1)}, bf16[512,128]{1,0:T(8,128)(2,1)}, u32[]{:S(2)}) copy-start(bf16[512,128]{1,0:T(8,128)(2,1)} %param.12) | copy-start | bytes 393220
  38.3 7.5 %copy-start.26 = (pred[576]{0:T(1024)(128)(4,1)S(1)}, pred[576]{0:T(1024)(128)(4,1)}, u32[]{:S(2)}) copy-start(pred[576]{0:T(1024)(128)(4,1)} %copy-done.25) | copy-start | bytes 1732
  38.3 0.6 copy-start.31
  38.9 0.8 copy-start.11
  38.9 8.8 %copy-start.3 = (bf16[576,1,8,64]{3,2,0,1:T(8,128)(2,1)S(1)}, bf16[576,1,8,64]{3,2,0,1:T(8,128)(2,1)}, u32[]{:S(2)}) copy-start(bf16[576,1,8,64]{3,2,0,1:T(8,128)(2,1)} %copy-done.2) | copy-start | bytes 1769476
  38.9 8.8 %copy-start.5 = (bf16[576,1,8,64]{3,2,0,1:T(8,128)(2,1)S(1)}, bf16[576,1,8,64]{3,2,0,1:T(8,128)(2,1)}, u32[]{:S(2)}) copy-start(bf16[576,1,8,64]{3,2,0,1:T(8,128)(2,1)} %copy-done.4) | copy-start | bytes 1769476
  39.7 10.9 %copy-start.8 = (f32[132096]{0:T(1024)}, f32[132096]{0:T(1024)S(1)}, u32[]{:S(2)}) copy-start(f32[132096]{0:T(1024)S(1)} %pad_maximum_fusion.3) | copy-start | bytes 1585156
  39.7 15.2 %collective-permute-start.2 = (f32[132096]{0:T(1024)S(1)}, f32[132096]{0:T(1024)S(1)}, u32[]{:S(2)}, u32[]{:S(2)}) collective-permute-start(f32[132096]{0:T(1024)S(1)} %pad_maximum_fusion.3), channel_id=1, source_target_pairs={{0,8},{8,16},{16,24},{24,32},{32,40},{40,48},{48,56},{1,9},{9,17},... | collective-permute-start | bytes 1585160 | tf_op jit(solution)/shard_map/ppermute | solution.py:16
  54.9 1.7 copy-start.9
  54.9 92.9 %all-reduce.2.cloned.1.call-start = ((), (), s32[]{:S(2)}) async-start(), calls=%async_computation.1 | async-start | bytes 1056768 | tf_op jit(solution)/shard_map/psum | solution.py:122
  58.8 2.0 copy-start.18
  58.8 2.0 copy-start.19
  64.5 5.9 %copy-start.14 = (bf16[512,1,64]{0,2,1:T(8,128)(2,1)S(1)}, bf16[512,1,64]{0,2,1:T(8,128)(2,1)}, u32[]{:S(2)}) copy-start(bf16[512,1,64]{0,2,1:T(8,128)(2,1)} %copy-done.13) | copy-start | bytes 196612
  64.5 5.9 %copy-start.16 = (bf16[512,1,64]{0,2,1:T(8,128)(2,1)S(1)}, bf16[512,1,64]{0,2,1:T(8,128)(2,1)}, u32[]{:S(2)}) copy-start(bf16[512,1,64]{0,2,1:T(8,128)(2,1)} %copy-done.15) | copy-start | bytes 196612
  64.5 5.9 %copy-start.24 = (bf16[64,1,128]{0,2,1:T(8,128)(2,1)S(1)}, bf16[64,1,128]{0,2,1:T(8,128)(2,1)}, u32[]{:S(2)}) copy-start(bf16[64,1,128]{0,2,1:T(8,128)(2,1)} %copy-done.23) | copy-start | bytes 49156
  68.4 90.1 %collective-permute-start.3 = (f32[132096]{0:T(1024)}, f32[132096]{0:T(1024)}, u32[]{:S(2)}, u32[]{:S(2)}) collective-permute-start(f32[132096]{0:T(1024)} %fusion.107), channel_id=1, source_target_pairs={{0,16},{8,24},{16,32},{24,40},{32,48},{40,56},{1,17},{9,25},{17,33... | collective-permute-start | bytes 1585160 | tf_op jit(solution)/shard_map/ppermute | solution.py:16
  70.4 7.2 %copy-start.6 = (pred[512,576]{0,1:T(8,128)(4,1)S(1)}, pred[512,576]{0,1:T(8,128)(4,1)}, u32[]{:S(2)}) copy-start(pred[512,576]{0,1:T(8,128)(4,1)} %get-tuple-element.29) | copy-start | bytes 884740
  73.9 3.7 %copy-start.1 = (f32[576,512,8]{1,0,2:T(8,128)}, f32[576,512,8]{1,0,2:T(8,128)S(1)}, u32[]{:S(2)}) copy-start(f32[576,512,8]{1,0,2:T(8,128)S(1)} %get-tuple-element.35) | copy-start | bytes 28311556
  77.6 73.8 %copy-start.7 = (pred[512,576]{0,1:T(8,128)(4,1)S(1)}, pred[512,576]{0,1:T(8,128)(4,1)}, u32[]{:S(2)}) copy-start(pred[512,576]{0,1:T(8,128)(4,1)} %get-tuple-element.29) | copy-start | bytes 884740
  77.6 73.8 %copy-start.28 = (bf16[512,128]{1,0:T(8,128)(2,1)S(1)}, bf16[512,128]{1,0:T(8,128)(2,1)}, u32[]{:S(2)}) copy-start(bf16[512,128]{1,0:T(8,128)(2,1)} %param.12) | copy-start | bytes 393220
  77.6 73.9 %copy-start.32 = (bf16[64,1,128]{2,0,1:T(8,128)(2,1)S(1)}, bf16[64,1,128]{2,0,1:T(8,128)(2,1)}, u32[]{:S(2)}) copy-start(bf16[64,1,128]{2,0,1:T(8,128)(2,1)} %copy-done.31) | copy-start | bytes 49156
  147.9 13.5 %copy-start.20 = (f32[132096]{0:T(1024)S(1)}, f32[132096]{0:T(1024)}, u32[]{:S(2)}) copy-start(f32[132096]{0:T(1024)} %all-reduce.2.cloned.1.call-done) | copy-start | bytes 1585156
  147.9 13.5 %collective-permute-start.5 = (f32[132096]{0:T(1024)}, f32[132096]{0:T(1024)S(1)}, u32[]{:S(2)}, u32[]{:S(2)}) collective-permute-start(f32[132096]{0:T(1024)} %all-reduce.2.cloned.1.call-done), channel_id=1, source_target_pairs={{0,64},{64,128},{128,192},{1,65},{65,129},{129,193},{2,66},{66,130... | collective-permute-start | bytes 1585160 | tf_op jit(solution)/shard_map/ppermute | solution.py:16
  158.6 7.7 %copy-start.17 = (f32[512,8,64]{0,2,1:T(8,128)S(1)}, f32[512,8,64]{0,2,1:T(8,128)}, u32[]{:S(2)}) copy-start(f32[512,8,64]{0,2,1:T(8,128)} %get-tuple-element.31) | copy-start | bytes 3145732
  159.9 6.7 %copy-start.12 = (bf16[576,8,128]{2,1,0:T(8,128)(2,1)S(1)}, bf16[576,8,128]{2,1,0:T(8,128)(2,1)}, u32[]{:S(2)}) copy-start(bf16[576,8,128]{2,1,0:T(8,128)(2,1)} %fusion.14) | copy-start | bytes 3538948
  159.9 6.7 %copy-start.21 = (pred[512,576]{0,1:T(8,128)(4,1)S(1)}, pred[512,576]{0,1:T(8,128)(4,1)}, u32[]{:S(2)}) copy-start(pred[512,576]{0,1:T(8,128)(4,1)} %get-tuple-element.28) | copy-start | bytes 884740
  159.9 26.0 %collective-permute-start.4 = (f32[132096]{0:T(1024)S(1)}, f32[132096]{0:T(1024)S(1)}, u32[]{:S(2)}, u32[]{:S(2)}) collective-permute-start(f32[132096]{0:T(1024)S(1)} %add.179), channel_id=1, source_target_pairs={{0,32},{8,40},{16,48},{24,56},{1,33},{9,41},{17,49},{25,57},{2,34}... | collective-permute-start | bytes 1585160 | tf_op jit(solution)/shard_map/ppermute | solution.py:16
  161.4 24.5 %collective-permute-start.6 = (f32[132096]{0:T(1024)S(1)}, f32[132096]{0:T(1024)S(1)}, u32[]{:S(2)}, u32[]{:S(2)}) collective-permute-start(f32[132096]{0:T(1024)S(1)} %add.181), channel_id=1, source_target_pairs={{0,128},{64,192},{1,129},{65,193},{2,130},{66,194},{3,131},{67,195... | collective-permute-start | bytes 1585160 | tf_op jit(solution)/shard_map/ppermute | solution.py:16
  166.6 19.3 %copy-start.10 = (f32[132096]{0:T(1024)S(1)}, f32[132096]{0:T(1024)}, u32[]{:S(2)}) copy-start(f32[132096]{0:T(1024)} %copy-done.9) | copy-start | bytes 1585156
  187.4 2.3 %copy-start.34 = (bf16[8,512,576]{1,2,0:T(8,128)(2,1)S(1)}, bf16[8,512,576]{1,2,0:T(8,128)(2,1)}, u32[]{:S(2)}) copy-start(bf16[8,512,576]{1,2,0:T(8,128)(2,1)} %get-tuple-element.37) | copy-start | bytes 14155780
  188.2 1.0 copy-start.29
  188.2 1.0 copy-start.30
  188.3 1.7 copy-start.22
  188.3 2.5 %copy-start.33 = (f32[128,8,512]{2,0,1:T(8,128)S(1)}, f32[128,8,512]{2,0,1:T(8,128)}, u32[]{:S(2)}) copy-start(f32[128,8,512]{2,0,1:T(8,128)} %fusion.10) | copy-start | bytes 6291460
Sparse Core Ops, SparseCore 0:
  66.5 81.3 all-reduce.1
where the time goes:
time: 222 us; the launch traced here: 221 us
  waiting for transfers between devices  88.4 us (40%)
  other arithmetic  34.5 us (16%)
  matrix products  22.5 us (10%)
  local copies, waits for them, and re-layouts  22.3 us (10%)
  blocking collectives  20.1 us (9%)
  starting transfers between devices  19.6 us (9%)
  between operations  14 us (6%)
    psum x1, waiting for transfers between devices, body(): row_total = lax.psum(packed, 'sz')  68.3 us
    all_to_all x1, blocking collectives, body(): lax.all_to_all(result, 'head', split_axis=0, concat_axis=1, tiled=True)  20.1 us
    ppermute x7, waiting for transfers between devices, passed_along(): lax.ppermute(value, axis, [(source, source + steps) for source in range(f...  20 us
    ppermute x7, starting transfers between devices, passed_along(): lax.ppermute(value, axis, [(source, source + steps) for source in range(f...  19.6 us
    unnamed x74, local copies, waits for them, and re-layouts  11.3 us
    dot_general x1, matrix products, body(): jnp.einsum('gkij,jgd->igkd', weights.astype(jnp.bfloat16), ext_values, pr...  7.13 us
    another operation x3, other arithmetic  5.46 us
  transfers between devices with their start and end apart: 8, of which 3 were waited for; matrix products, arithmetic and copies ran while one was open for 23% of the time, Pallas kernels for 0%

commit v1 on v0

--- a/solution.py
+++ b/solution.py
@@ -7,6 +7,11 @@
 WINDOW = 64
 BLOCK = 512
 SPAN = 256
+
+
+def detail_region(page, named_axis):
+    z2 = jax.lax.all_gather(page, named_axis)
+    return jnp.sum(z2, axis=0)
 
 
 def passed_along(value, axis, steps):
@@ -119,7 +124,7 @@
             steps *= 2
         return (exclusive, first)
 
-    row_total = lax.psum(packed, "sz")
+    row_total = detail_region(packed, "sz")
     inner, first_received = exclusive_scan(packed, "sz")
     outer, _ = exclusive_scan(row_total, "sx")
     exclusive = inner + outer

time: 222 us -> 207 us (0.932)
  waiting for transfers between devices: 88.4 us -> 63.4 us
  local copies, waits for them, and re-layouts: 22.3 us -> 26.2 us
  other arithmetic: 34.5 us -> 38 us
    psum x1 -> x0, waiting for transfers between devices: 68.3 us -> none  [body(): row_total = lax.psum(packed, 'sz')]
    all_gather x0 -> x1, waiting for transfers between devices: none -> 34.8 us  [detail_region(): z2 = jax.lax.all_gather(page, named_axis)]
    ppermute x7, waiting for transfers between devices: 20 us -> 28.6 us  [passed_along(): lax.ppermute(value, axis, [(source, source + steps) for source in range(f...]
    reduce_sum x0 -> x1, other arithmetic: none -> 7.07 us  [detail_region(): return jnp.sum(z2, axis=0)]
    all_gather x0 -> x1, local copies, waits for them, and re-layouts: none -> 4.77 us  [detail_region(): z2 = jax.lax.all_gather(page, named_axis)]
    unnamed x74 -> x64, local copies, waits for them, and re-layouts: 11.3 us -> 11.3 us
  transfers between devices with their start and end apart: 8 -> 8, of which waited for: 3 -> 4; matrix products, arithmetic and copies ran while one was open for 23% -> 33% of each run, Pallas kernels for 0% -> 0%
where the time goes in v1:
time: 207 us; the launch traced here: 205 us
  waiting for transfers between devices  63.4 us (31%)
  other arithmetic  38 us (18%)
  local copies, waits for them, and re-layouts  26.2 us (13%)
  matrix products  22.6 us (11%)
  starting transfers between devices  21 us (10%)
  blocking collectives  20.2 us (10%)
  between operations  14 us (7%)
    all_gather x1, waiting for transfers between devices, detail_region(): z2 = jax.lax.all_gather(page, named_axis)  34.8 us
    ppermute x7, waiting for transfers between devices, passed_along(): lax.ppermute(value, axis, [(source, source + steps) for source in range(f...  28.6 us
    ppermute x7, starting transfers between devices, passed_along(): lax.ppermute(value, axis, [(source, source + steps) for source in range(f...  21 us
    all_to_all x1, blocking collectives, body(): lax.all_to_all(result, 'head', split_axis=0, concat_axis=1, tiled=True)  20.2 us
    unnamed x64, local copies, waits for them, and re-layouts  11.3 us
    dot_general x1, matrix products, body(): jnp.einsum('gkij,jgd->igkd', weights.astype(jnp.bfloat16), ext_values, pr...  7.13 us
    reduce_sum x1, other arithmetic, detail_region(): return jnp.sum(z2, axis=0)  7.07 us
    another operation x3, other arithmetic  5.49 us
  transfers between devices with their start and end apart: 8, of which 4 were waited for; matrix products, arithmetic and copies ran while one was open for 33% of the time, Pallas kernels for 0%

profile of v1, /device:TPU:160, one launch (start us, length us, event | category | flops | bytes accessed | tf_op | source)
XLA Modules:
  0.0 205.4 jit_solution(12764744628151235673)
XLA Ops:
  6.5 0.8 add_bitcast_fusion
  7.3 1.0 copy.59
  8.4 2.4 %subtract_convert_fusion.3 = (bf16[512,1,64]{0,2,1:T(8,128)(2,1)S(1)}, bf16[512,1,64]{0,2,1:T(8,128)(2,1)S(1)}) fusion(f32[512,1,128]{0,2,1:T(8,128)S(1)} %bitcast_convert_fusion, f32[64]{0:T(128)} %constant.80.clone, f32[512]{0:T(512)S(1)} %get-tuple-element.27, f32[64]{0:T(128)} %constant.79.clone, f32[512]{0:T(512)S(1)} %get-tuple-element.26, ...), kind=kLoop, calls=%fused_computation.118 | loop fusion | flops 753664 | bytes 400128 | tf_op jit(solution)/shard_map/convert.6
  10.8 2.9 %collective-permute-start.1 = (bf16[64,1,128]{0,2,1:T(8,128)(2,1)S(1)}, bf16[64,1,128]{0,2,1:T(8,128)(2,1)S(1)}, u32[]{:S(2)}, u32[]{:S(2)}) collective-permute-start(bf16[64,1,128]{0,2,1:T(8,128)(2,1)S(1)} %pad_maximum_fusion.13), channel_id=1, source_target_pairs={{0,8},{8,16},{16,24},{24,32},{32,40},{40,48},{48,56},{56,64},{64,7... | collective-permute-start | bytes 49160 | tf_op jit(solution)/shard_map/ppermute | solution.py:21
  14.5 2.9 %collective-permute-start = (bf16[64,1,128]{2,0,1:T(8,128)(2,1)S(1)}, bf16[64,1,128]{2,0,1:T(8,128)(2,1)S(1)}, u32[]{:S(2)}, u32[]{:S(2)}) collective-permute-start(bf16[64,1,128]{2,0,1:T(8,128)(2,1)S(1)} %slice_bitcast_fusion), channel_id=1, source_target_pairs={{0,8},{8,16},{16,24},{24,32},{32,40},{40,48},{48,56},{56,64},{64,7... | collective-permute-start | bytes 49160 | tf_op jit(solution)/shard_map/ppermute | solution.py:21
  17.4 2.4 %fusion.58 = f32[576,512]{0,1} fusion(bf16[128,512]{0,1:T(8,128)(2,1)} %bitcast.177, bf16[512,1,64]{0,2,1:T(8,128)(2,1)S(1)} %get-tuple-element.22, bf16[512,1,64]{0,2,1:T(8,128)(2,1)S(1)} %get-tuple-element.21, bf16[64,1,128]{0,2,1:T(8,128)(2,1)S(1)} %collective-permute-done.1), kind=kOutput, calls=%fused_computation.99 | convolution fusion | flops 75939840 | bytes 1458176
  19.8 2.3 %copy.61 = f32[576,8,64]{2,1,0:T(8,128)S(1)} copy(f32[576,8,64]{0,2,1:T(8,128)} %bitcast.171) | data formatting | bytes 2359296 | tf_op jit(solution)/shard_map/ngd,gkdf->ngkf/dot_general | solution.py:88
  22.1 1.3 bitcast_reduce_fusion
  23.4 3.6 %fusion.25 = (f32[576,8]{1,0:T(8,128)S(1)}, f32[576,8]{1,0:T(8,128)S(1)}) fusion(f32[576,8,64]{2,1,0:T(8,128)S(1)} %copy.61, f32[576,8]{1,0:T(8,128)S(1)} %get-tuple-element.9, f32[576,8]{1,0:T(8,128)S(1)} %get-tuple-element.10), kind=kLoop, calls=%fused_computation.39 | loop fusion | flops 1465344 | bytes 1253376 | tf_op jit(solution)/shard_map/reduce_sum | solution.py:52
  27.0 3.1 %fusion.24 = (bf16[576,1,8,64]{3,2,0,1:T(8,128)(2,1)S(1)}, bf16[576,1,8,64]{3,2,0,1:T(8,128)(2,1)S(1)}) fusion(f32[576,8,64]{2,1,0:T(8,128)S(1)} %copy.61, f32[576,8]{1,0:T(8,128)S(1)} %get-tuple-element.7, f32[576,8]{1,0:T(8,128)S(1)} %get-tuple-element.9, f32[576,8]{1,0:T(8,128)S(1)} %get-tuple-element.8, f32[576,8]{1,0:T(8,128)S(1)} %get-tuple-element.10), kind=kLoop, calls=%fused_computation.38 | loop fusion | flops 2064384 | bytes 2433024 | tf_op jit(solution)/shard_map/div | solution.py:52
  30.2 4.0 %convert_reduce_fusion = (f32[8,128]{1,0:T(8,128)S(1)}, bf16[512,1,8,128]{3,2,0,1:T(8,128)(2,1)S(1)}) fusion(bf16[576,1,8,64]{3,2,0,1:T(8,128)(2,1)S(1)} %get-tuple-element.18, bf16[576,1,8,64]{3,2,0,1:T(8,128)(2,1)S(1)} %get-tuple-element.17, pred[512]{0:T(512)(128)(4,1)S(1)} %slice-done), kind=kLoop, calls=%fused_computation.34 | loop fusion | flops 3668992 | bytes 2232832 | tf_op jit(solution)/shard_map/reduce_sum | solution.py:99
  34.8 0.8 copy-done.12
  35.6 0.8 pad_maximum_fusion.3
  36.5 2.2 %fusion.64 = (f32[512,64]{0,1:T(8,128)}, f32[512,64]{0,1:T(8,128)S(1)}) fusion(f32[64]{0:T(128)S(1)} %copy-done.26, f32[512]{0:T(512)S(1)} %get-tuple-element.27, f32[64]{0:T(128)S(1)} %copy-done.25, f32[512]{0:T(512)S(1)} %get-tuple-element.26, f32[64]{0:T(128)S(1)} %copy-done.24, f32[512]{0:T(512)S(1)} %get-tuple-element.25), kind=kLoop, calls=%fused_computation.105 | loop fusion | flops 491520 | bytes 269056 | tf_op jit(solution)/shard_map/sub | solution.py:34
  38.7 2.1 %collective-permute-start.2 = (f32[132096]{0:T(1024)}, f32[132096]{0:T(1024)S(1)}, u32[]{:S(2)}, u32[]{:S(2)}) collective-permute-start(f32[132096]{0:T(1024)} %pad_maximum_fusion.3), channel_id=1, source_target_pairs={{0,8},{8,16},{16,24},{24,32},{32,40},{40,48},{48,56},{1,9},{9,17},... | collective-permute-start | bytes 1585160 | tf_op jit(solution)/shard_map/ppermute | solution.py:21
  40.8 1.7 copy.65
  42.5 0.9 copy.67
  43.4 1.1 fusion.33
  44.5 2.9 %fusion.14 = bf16[576,8,128]{2,1,0:T(8,128)(2,1)} fusion(bf16[576,8,64]{2,1,0:T(8,128)(2,1)S(1)} %bitcast.169, bf16[576,8,64]{2,1,0:T(8,128)(2,1)S(1)} %bitcast.168, pred[576]{0:T(1024)(128)(4,1)S(1)} %copy-done.21), kind=kLoop, calls=%fused_computation.18 | loop fusion | flops 2949120 | bytes 2359872 | tf_op jit(solution)/shard_map/convert_element_type | solution.py:91
  47.4 11.2 %collective-permute-done.2 = f32[132096]{0:T(1024)S(1)} collective-permute-done((f32[132096]{0:T(1024)}, f32[132096]{0:T(1024)S(1)}, u32[]{:S(2)}, u32[]{:S(2)}) %collective-permute-start.2) | collective-permute-done | bytes 528416 | tf_op jit(solution)/shard_map/ppermute | solution.py:21
  58.6 1.7 copy.63
  60.6 1.9 copy.87
  62.5 2.0 copy.88
  64.5 0.9 fusion.107
  65.3 2.1 %collective-permute-start.3 = (f32[132096]{0:T(1024)}, f32[132096]{0:T(1024)}, u32[]{:S(2)}, u32[]{:S(2)}) collective-permute-start(f32[132096]{0:T(1024)} %fusion.107), channel_id=1, source_target_pairs={{0,16},{8,24},{16,32},{24,40},{32,48},{40,56},{1,17},{9,25},{17,33... | collective-permute-start | bytes 1585160 | tf_op jit(solution)/shard_map/ppermute | solution.py:21
  67.4 2.8 %subtract_convert_fusion = (bf16[512,8,64]{2,0,1:T(8,128)(2,1)S(1)}, bf16[512,8,64]{2,0,1:T(8,128)(2,1)S(1)}) fusion(f32[512,8,64]{2,0,1:T(8,128)} %copy.88, f32[512,8,64]{2,0,1:T(8,128)} %copy.87, f32[512,64]{1,0:T(8,128)S(1)} %copy-done.17, f32[512,64]{1,0:T(8,128)S(1)} %copy-done.16), kind=kLoop, calls=%fused_computation.33 | loop fusion | flops 2097152 | bytes 3407872 | tf_op jit(solution)/shard_map/convert.4
  70.3 0.9 fusion.111
  71.1 1.9 fusion.110
  73.0 3.5 %fusion.2 = (f32[8,512]{1,0:T(8,128)S(1)}, f32[576,512,8]{1,0,2:T(8,128)S(1)}) fusion(pred[512,576]{0,1:T(8,128)(4,1)} %get-tuple-element.29, bf16[512,8,64]{2,0,1:T(8,128)(2,1)S(1)} %get-tuple-element.16, bf16[512,8,64]{2,0,1:T(8,128)(2,1)S(1)} %get-tuple-element.15, bf16[512,1,64]{0,2,1:T(8,128)(2,1)S(1)} %get-tuple-element.22, ...), kind=kOutput, calls=%fused_computation.4 | convolution fusion | flops 613593088 | bytes 10944512 | tf_op jit(solution)/shard_map/igkd,jgd->gkij/dot_general | solution.py:148
  76.5 3.6 %copy-done.2 = f32[576,512,8]{1,0,2:T(8,128)} copy-done((f32[576,512,8]{1,0,2:T(8,128)}, f32[576,512,8]{1,0,2:T(8,128)S(1)}, u32[]{:S(2)}) %copy-start.2) | copy-done | bytes 9437208
  80.1 1.9 fusion.5
  82.1 34.8 %all-gather.3.cloned.1.call-done = f32[1056768]{0:T(1024)} async-done(((f32[132096]{0:T(1024)}), f32[1056768]{0:T(1024)}) %all-gather.3.cloned.1.call-update) | async-done | bytes 4227088 | tf_op jit(solution)/shard_map/all_gather | solution.py:13
  116.8 4.8 %reshape.676 = f32[8,132096]{1,0:T(8,128)} reshape(f32[1056768]{0:T(1024)} %all-gather.3.cloned.1.call-done) | data formatting | bytes 8454144 | tf_op jit(solution)/shard_map/all_gather | solution.py:13
  121.6 7.1 %reduce_sum.87 = f32[132096]{0:T(1024)S(1)} reduce(f32[8,132096]{1,0:T(8,128)} %reshape.676, f32[]{:T(128)} %constant.76.clone.1), dimensions={0}, to_apply=%region_10.11 | reduce | flops 924672 | bytes 4755460 | tf_op jit(solution)/shard_map/reduce_sum | solution.py:14
  128.7 3.4 %collective-permute-start.5 = (f32[132096]{0:T(1024)S(1)}, f32[132096]{0:T(1024)S(1)}, u32[]{:S(2)}, u32[]{:S(2)}) collective-permute-start(f32[132096]{0:T(1024)S(1)} %reduce_sum.87), channel_id=1, source_target_pairs={{0,64},{64,128},{128,192},{1,65},{65,129},{129,193},{2,66},{66,130... | collective-permute-start | bytes 1585160 | tf_op jit(solution)/shard_map/ppermute | solution.py:21
  132.2 7.1 %fusion.10 = f32[128,8,512]{2,0,1:T(8,128)} fusion(f32[576,512,8]{1,0,2:T(8,128)} %copy-done.2, f32[8,512]{1,0:T(8,128)S(1)} %get-tuple-element.34, pred[512,576]{0,1:T(8,128)(4,1)S(1)} %copy-done.8, bf16[64,1,128]{2,0,1:T(8,128)(2,1)S(1)} %collective-permute-done, bf16[512,1,128]{2,0,1:T(8,128)(2,1)S(1)} %bitcast.182), kind=kOutput, calls=%fused_computation.14 | convolution fusion | flops 613711872 | bytes 11993088 | tf_op jit(solution)/shard_map/gkij,jgd->igkd/dot_general | solution.py:158
  139.3 1.3 add.177
  140.7 1.6 collective-permute-start.4
  142.3 1.2 collective-permute-done.5
  143.5 6.0 %collective-permute-start.6 = (f32[132096]{0:T(1024)S(1)}, f32[132096]{0:T(1024)S(1)}, u32[]{:S(2)}, u32[]{:S(2)}) collective-permute-start(f32[132096]{0:T(1024)S(1)} %add.179), channel_id=1, source_target_pairs={{0,128},{64,192},{1,129},{65,193},{2,130},{66,194},{3,131},{67,195... | collective-permute-start | bytes 1585160 | tf_op jit(solution)/shard_map/ppermute | solution.py:21
  149.8 3.6 %select_reduce_fusion = (f32[8,512]{1,0:T(8,128)S(1)}, bf16[8,512,576]{1,2,0:T(8,128)(2,1)}) fusion(pred[512,576]{0,1:T(8,128)(4,1)S(1)} %copy-done.18, bf16[512,8,64]{0,2,1:T(8,128)(2,1)S(1)} %get-tuple-element.38, bf16[512,8,64]{0,2,1:T(8,128)(2,1)S(1)} %get-tuple-element.39, bf16[576,8,128]{2,1,0:T(8,128)(2,1)S(1)} %copy-done.14), kind=kOutput, calls=%fused_computation.7 | convolution fusion | flops 613150720 | bytes 7258112 | tf_op jit(solution)/shard_map/igkf,jgkf->gkij/dot_general | solution.py:155
  153.5 16.2 %collective-permute-done.4 = f32[132096]{0:T(1024)S(1)} collective-permute-done((f32[132096]{0:T(1024)S(1)}, f32[132096]{0:T(1024)S(1)}, u32[]{:S(2)}, u32[]{:S(2)}) %collective-permute-start.4) | collective-permute-done | bytes 528416 | tf_op jit(solution)/shard_map/ppermute | solution.py:21
  169.7 1.2 add_add_fusion
  172.6 0.9 copy-done.29
  174.5 1.4 fusion.21
  175.9 0.8 copy.75
  177.2 20.2 %all_to_all.19 = bf16[8,64,1024]{2,1,0:T(8,128)(2,1)S(1)} all-to-all(bf16[8,64,1024]{2,1,0:T(8,128)(2,1)S(1)} %all_to_all.14), channel_id=1, replica_groups=mesh['sx'=4,'sz'=8,'head'=8] {'head'}, dimensions={0} | all-to-all | bytes 2097152 | tf_op jit(solution)/shard_map/all_to_all | solution.py:191
  197.5 1.1 copy.89
  (87 shorter events, 5.3 us)
Async XLA Ops:
  6.5 63.7 %copy-start = (bf16[8,128,64]{1,2,0:T(8,128)(2,1)S(1)}, bf16[8,128,64]{1,2,0:T(8,128)(2,1)}, u32[]{:S(2)}) copy-start(bf16[8,128,64]{1,2,0:T(8,128)(2,1)} %param.14) | copy-start | bytes 393220
  6.5 110.3 %all-gather.3.cloned.1.call-start = ((), (), s32[]{:S(2)}) async-start(), calls=%async_computation.1 | async-start | bytes 4755456 | tf_op jit(solution)/shard_map/all_gather | solution.py:13
  10.8 6.6 %collective-permute-start.1 = (bf16[64,1,128]{0,2,1:T(8,128)(2,1)S(1)}, bf16[64,1,128]{0,2,1:T(8,128)(2,1)S(1)}, u32[]{:S(2)}, u32[]{:S(2)}) collective-permute-start(bf16[64,1,128]{0,2,1:T(8,128)(2,1)S(1)} %pad_maximum_fusion.13), channel_id=1, source_target_pairs={{0,8},{8,16},{16,24},{24,32},{32,40},{40,48},{48,56},{56,64},{64,7... | collective-permute-start | bytes 49160 | tf_op jit(solution)/shard_map/ppermute | solution.py:21
  14.5 19.8 %collective-permute-start = (bf16[64,1,128]{2,0,1:T(8,128)(2,1)S(1)}, bf16[64,1,128]{2,0,1:T(8,128)(2,1)S(1)}, u32[]{:S(2)}, u32[]{:S(2)}) collective-permute-start(bf16[64,1,128]{2,0,1:T(8,128)(2,1)S(1)} %slice_bitcast_fusion), channel_id=1, source_target_pairs={{0,8},{8,16},{16,24},{24,32},{32,40},{40,48},{48,56},{56,64},{64,7... | collective-permute-start | bytes 49160 | tf_op jit(solution)/shard_map/ppermute | solution.py:21
  17.4 4.7 %copy-start.20 = (pred[576]{0:T(1024)(128)(4,1)}, pred[576]{0:T(1024)(128)(4,1)S(1)}, u32[]{:S(2)}) copy-start(pred[576]{0:T(1024)(128)(4,1)S(1)} %fusion.85) | copy-start | bytes 1732
  27.0 3.2 %slice-start = ((pred[576]{0:T(1024)(128)(4,1)}), pred[512]{0:T(512)(128)(4,1)S(1)}, s32[]{:S(2)}) async-start(pred[576]{0:T(1024)(128)(4,1)} %copy-done.20), calls=%async_computation.2 | async-start | bytes 1024 | tf_op jit(solution)/shard_map/slice | solution.py:94
  30.2 4.6 %copy-start.3 = (bf16[576,1,8,64]{3,2,0,1:T(8,128)(2,1)}, bf16[576,1,8,64]{3,2,0,1:T(8,128)(2,1)S(1)}, u32[]{:S(2)}) copy-start(bf16[576,1,8,64]{3,2,0,1:T(8,128)(2,1)S(1)} %get-tuple-element.17) | copy-start | bytes 1769476
  30.2 4.6 %copy-start.5 = (bf16[576,1,8,64]{3,2,0,1:T(8,128)(2,1)}, bf16[576,1,8,64]{3,2,0,1:T(8,128)(2,1)S(1)}, u32[]{:S(2)}) copy-start(bf16[576,1,8,64]{3,2,0,1:T(8,128)(2,1)S(1)} %get-tuple-element.18) | copy-start | bytes 1769476
  30.2 4.1 %copy-start.22 = (bf16[512,128]{1,0:T(8,128)(2,1)S(1)}, bf16[512,128]{1,0:T(8,128)(2,1)}, u32[]{:S(2)}) copy-start(bf16[512,128]{1,0:T(8,128)(2,1)} %param.12) | copy-start | bytes 393220
  34.2 2.2 %copy-start.27 = (f32[8]{0:T(128)S(1)}, f32[8]{0:T(128)}, u32[]{:S(2)}) copy-start(f32[8]{0:T(128)} %param.16) | copy-start | bytes 100
  34.2 2.3 %copy-start.24 = (f32[64]{0:T(128)S(1)}, f32[64]{0:T(128)}, u32[]{:S(2)}) copy-start(f32[64]{0:T(128)} %constant.78.clone) | copy-start | bytes 772
  34.2 2.3 %copy-start.25 = (f32[64]{0:T(128)S(1)}, f32[64]{0:T(128)}, u32[]{:S(2)}) copy-start(f32[64]{0:T(128)} %constant.79.clone) | copy-start | bytes 772
  34.2 2.3 %copy-start.26 = (f32[64]{0:T(128)S(1)}, f32[64]{0:T(128)}, u32[]{:S(2)}) copy-start(f32[64]{0:T(128)} %constant.80.clone) | copy-start | bytes 772
  34.2 9.1 %copy-start.21 = (pred[576]{0:T(1024)(128)(4,1)S(1)}, pred[576]{0:T(1024)(128)(4,1)}, u32[]{:S(2)}) copy-start(pred[576]{0:T(1024)(128)(4,1)} %copy-done.20) | copy-start | bytes 1732
  34.8 0.8 copy-start.12
  34.8 9.7 %copy-start.4 = (bf16[576,1,8,64]{3,2,0,1:T(8,128)(2,1)S(1)}, bf16[576,1,8,64]{3,2,0,1:T(8,128)(2,1)}, u32[]{:S(2)}) copy-start(bf16[576,1,8,64]{3,2,0,1:T(8,128)(2,1)} %copy-done.3) | copy-start | bytes 1769476
  34.8 9.7 %copy-start.6 = (bf16[576,1,8,64]{3,2,0,1:T(8,128)(2,1)S(1)}, bf16[576,1,8,64]{3,2,0,1:T(8,128)(2,1)}, u32[]{:S(2)}) copy-start(bf16[576,1,8,64]{3,2,0,1:T(8,128)(2,1)} %copy-done.5) | copy-start | bytes 1769476
  38.7 19.9 %collective-permute-start.2 = (f32[132096]{0:T(1024)}, f32[132096]{0:T(1024)S(1)}, u32[]{:S(2)}, u32[]{:S(2)}) collective-permute-start(f32[132096]{0:T(1024)} %pad_maximum_fusion.3), channel_id=1, source_target_pairs={{0,8},{8,16},{16,24},{24,32},{32,40},{40,48},{48,56},{1,9},{9,17},... | collective-permute-start | bytes 1585160 | tf_op jit(solution)/shard_map/ppermute | solution.py:21
  58.6 1.7 copy-start.9
  62.5 2.0 copy-start.10
  62.5 2.0 copy-start.13
  62.5 4.9 %copy-start.16 = (f32[512,64]{1,0:T(8,128)S(1)}, f32[512,64]{1,0:T(8,128)}, u32[]{:S(2)}) copy-start(f32[512,64]{1,0:T(8,128)} %copy.65) | copy-start | bytes 393220
  62.5 4.9 %copy-start.17 = (f32[512,64]{1,0:T(8,128)S(1)}, f32[512,64]{1,0:T(8,128)}, u32[]{:S(2)}) copy-start(f32[512,64]{1,0:T(8,128)} %copy.67) | copy-start | bytes 393220
  65.3 74.0 %collective-permute-start.3 = (f32[132096]{0:T(1024)}, f32[132096]{0:T(1024)}, u32[]{:S(2)}, u32[]{:S(2)}) collective-permute-start(f32[132096]{0:T(1024)} %fusion.107), channel_id=1, source_target_pairs={{0,16},{8,24},{16,32},{24,40},{32,48},{40,56},{1,17},{9,25},{17,33... | collective-permute-start | bytes 1585160 | tf_op jit(solution)/shard_map/ppermute | solution.py:21
  73.0 7.1 %copy-start.7 = (pred[512,576]{0,1:T(8,128)(4,1)S(1)}, pred[512,576]{0,1:T(8,128)(4,1)}, u32[]{:S(2)}) copy-start(pred[512,576]{0,1:T(8,128)(4,1)} %get-tuple-element.29) | copy-start | bytes 884740
  76.5 3.7 %copy-start.2 = (f32[576,512,8]{1,0,2:T(8,128)}, f32[576,512,8]{1,0,2:T(8,128)S(1)}, u32[]{:S(2)}) copy-start(f32[576,512,8]{1,0,2:T(8,128)S(1)} %get-tuple-element.35) | copy-start | bytes 28311556
  121.6 10.5 %copy-start.8 = (pred[512,576]{0,1:T(8,128)(4,1)S(1)}, pred[512,576]{0,1:T(8,128)(4,1)}, u32[]{:S(2)}) copy-start(pred[512,576]{0,1:T(8,128)(4,1)} %get-tuple-element.29) | copy-start | bytes 884740
  121.6 10.5 %copy-start.23 = (bf16[512,128]{1,0:T(8,128)(2,1)S(1)}, bf16[512,128]{1,0:T(8,128)(2,1)}, u32[]{:S(2)}) copy-start(bf16[512,128]{1,0:T(8,128)(2,1)} %param.12) | copy-start | bytes 393220
  128.7 14.8 %collective-permute-start.5 = (f32[132096]{0:T(1024)S(1)}, f32[132096]{0:T(1024)S(1)}, u32[]{:S(2)}, u32[]{:S(2)}) collective-permute-start(f32[132096]{0:T(1024)S(1)} %reduce_sum.87), channel_id=1, source_target_pairs={{0,64},{64,128},{128,192},{1,65},{65,129},{129,193},{2,66},{66,130... | collective-permute-start | bytes 1585160 | tf_op jit(solution)/shard_map/ppermute | solution.py:21
  139.3 10.2 %copy-start.15 = (f32[512,8,64]{0,2,1:T(8,128)S(1)}, f32[512,8,64]{0,2,1:T(8,128)}, u32[]{:S(2)}) copy-start(f32[512,8,64]{0,2,1:T(8,128)} %get-tuple-element.31) | copy-start | bytes 3145732
  140.6 9.2 %copy-start.14 = (bf16[576,8,128]{2,1,0:T(8,128)(2,1)S(1)}, bf16[576,8,128]{2,1,0:T(8,128)(2,1)}, u32[]{:S(2)}) copy-start(bf16[576,8,128]{2,1,0:T(8,128)(2,1)} %fusion.14) | copy-start | bytes 3538948
  140.6 9.2 %copy-start.18 = (pred[512,576]{0,1:T(8,128)(4,1)S(1)}, pred[512,576]{0,1:T(8,128)(4,1)}, u32[]{:S(2)}) copy-start(pred[512,576]{0,1:T(8,128)(4,1)} %get-tuple-element.28) | copy-start | bytes 884740
  140.7 29.0 %collective-permute-start.4 = (f32[132096]{0:T(1024)S(1)}, f32[132096]{0:T(1024)S(1)}, u32[]{:S(2)}, u32[]{:S(2)}) collective-permute-start(f32[132096]{0:T(1024)S(1)} %add.177), channel_id=1, source_target_pairs={{0,32},{8,40},{16,48},{24,56},{1,33},{9,41},{17,49},{25,57},{2,34}... | collective-permute-start | bytes 1585160 | tf_op jit(solution)/shard_map/ppermute | solution.py:21
  143.5 26.2 %collective-permute-start.6 = (f32[132096]{0:T(1024)S(1)}, f32[132096]{0:T(1024)S(1)}, u32[]{:S(2)}, u32[]{:S(2)}) collective-permute-start(f32[132096]{0:T(1024)S(1)} %add.179), channel_id=1, source_target_pairs={{0,128},{64,192},{1,129},{65,193},{2,130},{66,194},{3,131},{67,195... | collective-permute-start | bytes 1585160 | tf_op jit(solution)/shard_map/ppermute | solution.py:21
  149.8 19.9 %copy-start.11 = (f32[132096]{0:T(1024)S(1)}, f32[132096]{0:T(1024)}, u32[]{:S(2)}) copy-start(f32[132096]{0:T(1024)} %copy-done.9) | copy-start | bytes 1585156
  171.2 2.3 %copy-start.29 = (bf16[8,512,576]{1,2,0:T(8,128)(2,1)S(1)}, bf16[8,512,576]{1,2,0:T(8,128)(2,1)}, u32[]{:S(2)}) copy-start(bf16[8,512,576]{1,2,0:T(8,128)(2,1)} %get-tuple-element.37) | copy-start | bytes 14155780
  172.0 1.7 copy-start.19
  172.0 2.5 %copy-start.28 = (f32[128,8,512]{2,0,1:T(8,128)S(1)}, f32[128,8,512]{2,0,1:T(8,128)}, u32[]{:S(2)}) copy-start(f32[128,8,512]{2,0,1:T(8,128)} %fusion.10) | copy-start | bytes 6291460
  176.7 21.8 %copy-start.1 = (bf16[8,128,64]{1,2,0:T(8,128)(2,1)S(1)}, bf16[8,128,64]{1,2,0:T(8,128)(2,1)}, u32[]{:S(2)}) copy-start(bf16[8,128,64]{1,2,0:T(8,128)(2,1)} %param.14) | copy-start | bytes 393220
Sparse Core Ops, SparseCore 0:
  36.5 80.2 all-gather.2
